TPU v7x, 256 devices: a whole 4x4x8 slice. The times are simulated.
256 devices in a mesh: segment: 4 (over x), dp: 64 (over z, y, core).
Axes of the slice: x: 4, y: 4, z: 8, core: 2. Of those that a mesh axis runs over, the one named last changes fastest.
Arguments:
- x_saved: bfloat16 [4, 8192, 1536], P('segment', 'dp'), may hold values from -6 to 6
- gains: float32 [4, 1536], P('segment'), may hold values from 0.1 to 1.9
- w_in: bfloat16 [4, 1536, 3072], P('segment', 'dp'), may hold values from -0.15625 to 0.15625
- w_out: bfloat16 [4, 3072, 1536], P('segment', None, 'dp'), may hold values from -0.109375 to 0.109375
- cotangent: bfloat16 [8192, 1536], P('dp'), may hold values from -6 to 6
- lengths: int32 [64], replicated, may hold values from 1 to 256, 8192 in all
Outputs:
- grads: bfloat16 [4, 8192, 1536], P('segment', 'dp')
- gain_grads: float32 [4, 1536], P('segment')
All inputs are finite; a program needn't handle non-finite values.
Results may differ from a plain program's by a relative error of at most 0.0075.
Values may be sent and summed in bfloat16 or wider, within the bound.
No kernel may reach another device: no remote copies, remote signals or barrier semaphores. Data moves between devices by JAX's collectives and lax.ppermute only.
A program may use at most 128 MiB of HBM per device.

v0:
```python
import jax
import jax.numpy as jnp
from jax import lax
import numpy as np
from jax.sharding import Mesh, PartitionSpec as P

DP = ("z", "y", "core")


def passed_along(x, axis, by):
    length = lax.axis_size(axis)
    pairs = [(i, i + by) for i in range(length) if 0 <= i + by < length]
    return lax.ppermute(x, axis, pairs)


def on_device(x_saved, gains, w_in, w_out, cotangent, lengths):
    rows = cotangent.shape[0]
    width = cotangent.shape[1]
    ends = jnp.cumsum(lengths)
    position = lax.axis_index(DP) * rows + jnp.arange(rows, dtype=jnp.int32)
    utter_hit = (position[:, None] >= ends[None, :]).astype(jnp.int32)
    utter = jnp.sum(utter_hit, 1)
    onehot = (utter[:, None] == jnp.arange(lengths.shape[0], dtype=jnp.int32)[None, :]).astype(
        jnp.int32
    )
    tok_len = jnp.sum(onehot * lengths[None, :], 1).astype(jnp.float32)
    weight = 2.0 * rows / (tok_len + rows)
    current = (cotangent.astype(jnp.float32) * weight[:, None]).astype(jnp.bfloat16)
    xf = x_saved[0].astype(jnp.float32)
    centered_input = xf - jnp.mean(xf, -1, keepdims=True)
    variance = jnp.mean(centered_input * centered_input, -1, keepdims=True)
    inverse_deviation = lax.rsqrt(variance + 1e-05)
    standardized_input = centered_input * inverse_deviation
    gain_vector = gains[0]
    normalized_input = (standardized_input * gain_vector).astype(jnp.bfloat16)
    w_first, w_second = (
        lax.all_gather(w_in[0], DP, axis=0, tiled=True),
        lax.all_gather(w_out[0], DP, axis=1, tiled=True),
    )

    def project_all(normed_rows, grad_in):
        hidden = jnp.dot(normed_rows, w_first, preferred_element_type=jnp.float32)
        up_grad = jnp.dot(grad_in, w_second.T, preferred_element_type=jnp.float32)
        sig = jax.nn.sigmoid(hidden)
        hid_grad = (0.5 * up_grad * (sig + hidden * sig * (1.0 - sig))).astype(jnp.bfloat16)
        return jnp.dot(hid_grad, w_first.T, preferred_element_type=jnp.float32)

    def block_back():

        def run(grad_in):
            norm_gradient = project_all(normalized_input, grad_in)
            gain_partial = jnp.sum(norm_gradient * standardized_input, 0)
            gain_scaled = norm_gradient * gain_vector
            backward_result = inverse_deviation * (
                gain_scaled
                - jnp.mean(gain_scaled, -1, keepdims=True)
                - standardized_input * jnp.mean(gain_scaled * standardized_input, -1, keepdims=True)
            )
            return (
                (grad_in.astype(jnp.float32) + backward_result).astype(jnp.bfloat16),
                gain_partial,
            )

        return run

    def pass_through(grad_in):
        return (grad_in, jnp.zeros((width,), jnp.float32))

    segments = lax.axis_size("segment")
    my_segment = lax.axis_index("segment")
    gain_local = jnp.zeros((width,), jnp.float32)
    result = current
    for level in range(segments - 1, -1, -1):
        mine = my_segment == level
        updated, gain_partial = lax.cond(mine, block_back(), pass_through, current)
        result = jnp.where(mine, updated, result)
        gain_local = jnp.where(mine, gain_partial, gain_local)
        if level > 0:
            current = passed_along(updated, "segment", -1)
    gain_total = lax.psum(lax.psum(lax.psum(gain_local, "core"), "y"), "z")
    return (result[None], gain_total[None])


def solution(mesh):
    n_seg, n_dp = mesh.devices.shape
    sizes = dict(zip(("z", "y", "core"), (n_dp // 8, 4, 2)))
    mesh = Mesh(
        np.asarray(mesh.devices).reshape(n_seg, sizes["z"], sizes["y"], sizes["core"]),
        ("segment",) + DP,
    )
    in_specs = (
        P("segment", DP, None),
        P("segment", None),
        P("segment", DP, None),
        P("segment", None, DP),
        P(DP, None),
        P(),
    )
    out_specs = (P("segment", DP, None), P("segment", None))
    return jax.shard_map(
        on_device, mesh=mesh, in_specs=in_specs, out_specs=out_specs, check_vma=False
    )
```

profile of v0, /device:TPU:8, one launch (start us, length us, event | category | flops | bytes accessed | tf_op | source)
XLA Modules:
  0.0 332.8 jit_solution(8786208565369843301)
XLA Ops:
  7.2 0.7 all-gather.7.cloned.1.call-update
  7.9 0.0 all-gather.5.cloned.1.call-start
  7.9 0.7 all-gather.5.cloned.1.call-update
  8.7 0.7 copy.17
  9.4 0.1 reduce-window.8
  9.5 0.1 reduce.5
  9.6 0.7 reduce.6
  10.4 0.1 convert_reduce_fusion.1
  10.4 0.7 select_reduce_fusion
  11.2 1.1 convert_reduce_fusion
  12.3 1.2 fusion.23
  13.6 1.5 fusion.21
  15.1 81.4 %all-gather.7.cloned.1.call-done = bf16[1,1536,3072]{2,1,0:T(8,128)(2,1)} async-done(((bf16[1,24,3072]{2,1,0:T(8,128)(2,1)}), bf16[1,1536,3072]{2,1,0:T(8,128)(2,1)}) %all-gather.7.cloned.1.call-update) | async-done | bytes 9437200 | tf_op jit(solution)/shard_map/all_gather | solution.py:37
  96.5 84.1 %all-gather.5.cloned.1.call-done = bf16[1,3072,1536]{1,2,0:T(8,128)(2,1)} async-done(((bf16[1,3072,24]{1,2,0:T(8,128)(2,1)}), bf16[1,3072,1536]{1,2,0:T(8,128)(2,1)}) %all-gather.5.cloned.1.call-update) | async-done | bytes 9437200 | tf_op jit(solution)/shard_map/all_gather | solution.py:38
  180.6 0.6 conditional.4
  180.7 0.6 broadcast.129
  181.2 1.3 collective-permute-start
  182.5 11.9 %collective-permute-done = bf16[128,1536]{1,0:T(8,128)(2,1)S(1)} collective-permute-done((bf16[128,1536]{1,0:T(8,128)(2,1)S(1)}, bf16[128,1536]{1,0:T(8,128)(2,1)S(1)}, u32[]{:S(2)}, u32[]{:S(2)}) %collective-permute-start) | collective-permute-done | bytes 393248 | tf_op jit(solution)/shard_map/ppermute | solution.py:13
  194.4 1.3 collective-permute-start.1
  195.7 11.0 %collective-permute-done.1 = bf16[128,1536]{1,0:T(8,128)(2,1)S(1)} collective-permute-done((bf16[128,1536]{1,0:T(8,128)(2,1)S(1)}, bf16[128,1536]{1,0:T(8,128)(2,1)S(1)}, u32[]{:S(2)}, u32[]{:S(2)}) %collective-permute-start.1) | collective-permute-done | bytes 393248 | tf_op jit(solution)/shard_map/ppermute | solution.py:13
  206.7 0.6 conditional.6
  206.7 0.6 broadcast.137
  207.3 1.3 collective-permute-start.2
  208.6 66.9 %collective-permute-done.2 = bf16[128,1536]{1,0:T(8,128)(2,1)S(1)} collective-permute-done((bf16[128,1536]{1,0:T(8,128)(2,1)S(1)}, bf16[128,1536]{1,0:T(8,128)(2,1)S(1)}, u32[]{:S(2)}, u32[]{:S(2)}) %collective-permute-start.2) | collective-permute-done | bytes 393248 | tf_op jit(solution)/shard_map/ppermute | solution.py:13
  275.4 20.4 %conditional.7 = (bf16[128,1536]{1,0:T(8,128)(2,1)S(1)}, f32[1536]{0:T(1024)S(1)}) conditional(s32[]{:T(128)} %convert_element_type.77, bf16[128,1536]{1,0:T(8,128)(2,1)S(1)} %collective-permute-done.2, (bf16[128,1536]{1,0:T(8,128)(2,1)S(1)}, f32[128,1]{0,1:T(1,128)}, bf16[3072,1536]{0,1:T(8,128)(2,1)}, bf16[128,1536]{1,0:T(8,128)(2,1)S(1)}, ...), branch_computations={%region_20.21_spmd, %region_21.25_spmd} | conditional | flops 3630562048 | bytes 36213296 | solution.py:75
  275.5 6.2 %fusion.28 = f32[128,3072]{1,0:T(8,128)} fusion(bf16[128,1536]{1,0:T(8,128)(2,1)S(1)} %get-tuple-element.84, bf16[1536,3072]{1,0:T(8,128)(2,1)} %get-tuple-element.85), kind=kOutput, calls=%fused_computation.69 | convolution fusion | flops 1207959552 | bytes 11403264 | tf_op jit(solution)/shard_map/cond/branch_1_fun/dot_general | solution.py:42
  281.7 12.7 %multiply_reduce_fusion.9 = (f32[1536]{0:T(1024)S(1)}, f32[128]{0:T(128)S(1)}, f32[128]{0:T(128)S(1)}, f32[128,1536]{1,0:T(8,128)}) fusion(f32[128,1536]{1,0:T(8,128)S(1)} %get-tuple-element.87, f32[1536]{0:T(1024)S(1)} %reduce.4, bf16[1536,3072]{1,0:T(8,128)(2,1)} %get-tuple-element.85, bf16[128,1536]{1,0:T(8,128)(2,1)S(1)} %get-tuple-element.81, ...), kind=kOutput, calls=%fused_computation.39 | convolution fusion | flops 2421029376 | bytes 22426624 | tf_op jit(solution)/shard_map/cond/branch_1_fun/dot_general | solution.py:46
  294.4 1.4 add_convert_fusion.3
  295.9 0.8 select_bitcast_fusion
  296.7 2.5 psum.21
  299.2 9.6 %psum.22 = f32[1536]{0:T(1024)S(1)} all-reduce(f32[1536]{0:T(1024)S(1)} %psum.21), channel_id=1, replica_groups=mesh['segment'=4,'z'=8,'y'=4,'core'=2] {'y'}, use_global_device_ids=true, to_apply=%region_26.27 | all-reduce | flops 1536 | bytes 12288 | tf_op jit(solution)/shard_map/psum | solution.py:80
  308.9 17.1 %psum.23 = f32[1,1536]{1,0:T(1,128)} all-reduce(f32[1,1536]{1,0:T(1,128)S(1)} %broadcast_in_dim.5), channel_id=1, replica_groups=mesh['segment'=4,'z'=8,'y'=4,'core'=2] {'z'}, use_global_device_ids=true, to_apply=%region_27.28 | all-reduce | flops 1536 | bytes 12288 | tf_op jit(solution)/shard_map/psum | solution.py:80
  (22 shorter events, 0.2 us)
Async XLA Ops:
  7.2 89.4 %all-gather.7.cloned.1.call-start = ((), (), s32[]{:S(2)}) async-start(), calls=%async_computation.1 | async-start | bytes 9584640 | tf_op jit(solution)/shard_map/all_gather | solution.py:37
  7.9 172.7 %all-gather.5.cloned.1.call-start = ((), (), s32[]{:S(2)}) async-start(), calls=%async_computation | async-start | bytes 9584640 | tf_op jit(solution)/shard_map/all_gather | solution.py:38
  11.2 169.4 %copy-start = (f32[1,1536]{1,0:T(1,128)S(1)}, f32[1,1536]{1,0:T(1,128)}, u32[]{:S(2)}) copy-start(f32[1,1536]{1,0:T(1,128)} %param.15) | copy-start | bytes 18436
  13.6 167.0 %copy-start.3 = (f32[128,1]{0,1:T(1,128)}, f32[128,1]{0,1:T(1,128)S(1)}, u32[]{:S(2)}) copy-start(f32[128,1]{0,1:T(1,128)S(1)} %get-tuple-element.189) | copy-start | bytes 1540
  181.2 13.2 %collective-permute-start = (bf16[128,1536]{1,0:T(8,128)(2,1)S(1)}, bf16[128,1536]{1,0:T(8,128)(2,1)S(1)}, u32[]{:S(2)}, u32[]{:S(2)}) collective-permute-start(bf16[128,1536]{1,0:T(8,128)(2,1)S(1)} %get-tuple-element.98), channel_id=1, source_target_pairs={{64,0},{128,64},{192,128},{65,1},{129,65},{193,129},{66,2},{130,66... | collective-permute-start | bytes 1179656 | tf_op jit(solution)/shard_map/ppermute | solution.py:13
  194.4 12.3 %copy-start.1 = (f32[1536]{0:T(1024)}, f32[1536]{0:T(1024)S(1)}, u32[]{:S(2)}) copy-start(f32[1536]{0:T(1024)S(1)} %get-tuple-element.104) | copy-start | bytes 18436
  194.4 12.3 %collective-permute-start.1 = (bf16[128,1536]{1,0:T(8,128)(2,1)S(1)}, bf16[128,1536]{1,0:T(8,128)(2,1)S(1)}, u32[]{:S(2)}, u32[]{:S(2)}) collective-permute-start(bf16[128,1536]{1,0:T(8,128)(2,1)S(1)} %get-tuple-element.99), channel_id=1, source_target_pairs={{64,0},{128,64},{192,128},{65,1},{129,65},{193,129},{66,2},{130,66... | collective-permute-start | bytes 1179656 | tf_op jit(solution)/shard_map/ppermute | solution.py:13
  207.3 68.2 %collective-permute-start.2 = (bf16[128,1536]{1,0:T(8,128)(2,1)S(1)}, bf16[128,1536]{1,0:T(8,128)(2,1)S(1)}, u32[]{:S(2)}, u32[]{:S(2)}) collective-permute-start(bf16[128,1536]{1,0:T(8,128)(2,1)S(1)} %get-tuple-element.100), channel_id=1, source_target_pairs={{64,0},{128,64},{192,128},{65,1},{129,65},{193,129},{66,2},{130,66... | collective-permute-start | bytes 1179656 | tf_op jit(solution)/shard_map/ppermute | solution.py:13
  281.7 12.7 %copy-start.6 = (f32[128,1]{0,1:T(1,128)S(1)}, f32[128,1]{0,1:T(1,128)}, u32[]{:S(2)}) copy-start(f32[128,1]{0,1:T(1,128)} %get-tuple-element.82) | copy-start | bytes 1540 | tf_op jit(solution)/shard_map/cond
  295.8 0.8 copy-start.2
Sparse Core Ops, SparseCore 0:
  10.7 85.7 all-gather.6
  99.3 81.3 all-gather.4
where the time goes:
time: 333 us
  waiting for transfers between devices  257 us (77%)
  blocking collectives  29.2 us (9%)
  matrix products  18.9 us (6%)
  between operations  14.2 us (4%)
  other arithmetic  7.94 us (2%)
  starting transfers between devices  3.92 us (1%)
    ppermute x3, waiting for transfers between devices, passed_along(): return lax.ppermute(x, axis, pairs)  89.7 us
    all_gather x1, waiting for transfers between devices, on_device(): lax.all_gather(w_out[0], DP, axis=1, tiled=True)  84.1 us
    all_gather x1, waiting for transfers between devices, on_device(): lax.all_gather(w_in[0], DP, axis=0, tiled=True)  81.4 us
    psum x3, blocking collectives, on_device(): gain_total = lax.psum(lax.psum(lax.psum(gain_local, 'core'), 'y'), 'z')  29.2 us
    dot_general x1, matrix products, project_all(): return jnp.dot(hid_grad, w_first.T, preferred_element_type=jnp.float32)  12.7 us
  transfers between devices with their start and end apart: 5, of which 5 were waited for; matrix products, arithmetic and copies ran while one was open for 2% of the time, Pallas kernels for 0%

commit v1 on v0

--- a/solution.py
+++ b/solution.py
@@ -35,7 +35,9 @@
     normalized_input = (standardized_input * gain_vector).astype(jnp.bfloat16)
     w_first, w_second = (
         lax.all_gather(w_in[0], DP, axis=0, tiled=True),
-        lax.all_gather(w_out[0], DP, axis=1, tiled=True),
+        jnp.concatenate(
+            lax.all_to_all(jnp.stack([w_out[0]] * lax.axis_size(DP)), DP, 0, 0), axis=1
+        ),
     )
 
     def project_all(normed_rows, grad_in):

time: 333 us -> 413 us (1.24)
  waiting for transfers between devices: 257 us -> 319 us
  starting transfers between devices: 3.92 us -> 16.3 us
  blocking collectives: 29.2 us -> 34.8 us
  other arithmetic: 7.94 us -> 3.47 us
    all_to_all x0 -> x1, waiting for transfers between devices: none -> 234 us  [on_device(): lax.all_to_all(jnp.stack([w_out[0]] * lax.axis_size(DP)), DP, 0, 0)]
    all_gather x1 -> x0, waiting for transfers between devices: 84.1 us -> none  [on_device(): lax.all_gather(w_out[0], DP, axis=1, tiled=True)]
    all_gather x1, waiting for transfers between devices: 81.4 us -> 0.01 us  [on_device(): lax.all_gather(w_in[0], DP, axis=0, tiled=True)]
    all_to_all x0 -> x1, starting transfers between devices: none -> 12.4 us  [on_device(): lax.all_to_all(jnp.stack([w_out[0]] * lax.axis_size(DP)), DP, 0, 0)]
    ppermute x3, waiting for transfers between devices: 89.7 us -> 83.8 us  [passed_along(): return lax.ppermute(x, axis, pairs)]
    psum x3, blocking collectives: 29.2 us -> 34.8 us  [on_device(): gain_total = lax.psum(lax.psum(lax.psum(gain_local, 'core'), 'y'), 'z')]
  transfers between devices with their start and end apart: 5 -> 5, of which waited for: 5 -> 4; matrix products, arithmetic and copies ran while one was open for 2% -> 0% of each run, Pallas kernels for 0% -> 0%
where the time goes in v1:
time: 413 us; the launch traced here: 412 us
  waiting for transfers between devices  319 us (77%)
  blocking collectives  34.8 us (8%)
  matrix products  18.9 us (5%)
  starting transfers between devices  16.3 us (4%)
  between operations  14.2 us (3%)
  local copies, waits for them, and re-layouts  5.97 us (1%)
    all_to_all x1, waiting for transfers between devices, on_device(): lax.all_to_all(jnp.stack([w_out[0]] * lax.axis_size(DP)), DP, 0, 0)  234 us
    ppermute x3, waiting for transfers between devices, passed_along(): return lax.ppermute(x, axis, pairs)  83.8 us
    psum x3, blocking collectives, on_device(): gain_total = lax.psum(lax.psum(lax.psum(gain_local, 'core'), 'y'), 'z')  34.8 us
    dot_general x1, matrix products, project_all(): return jnp.dot(hid_grad, w_first.T, preferred_element_type=jnp.float32)  12.7 us
    all_to_all x1, starting transfers between devices, on_device(): lax.all_to_all(jnp.stack([w_out[0]] * lax.axis_size(DP)), DP, 0, 0)  12.4 us
  transfers between devices with their start and end apart: 5, of which 4 were waited for; matrix products, arithmetic and copies ran while one was open for 0% of the time, Pallas kernels for 0%

profile of v1, /device:TPU:8, one launch (start us, length us, event | category | flops | bytes accessed | tf_op | source)
XLA Modules:
  0.0 412.3 jit_solution(10526616846172965345)
XLA Ops:
  7.2 5.8 %stack.3 = bf16[64,3072,24]{1,2,0:T(8,128)(2,1)} broadcast(bf16[3072,24]{0,1:T(8,128)(2,1)} %bitcast.50), dimensions={1,2} | broadcast | bytes 9584640 | tf_op jit(solution)/shard_map/stack | solution.py:39
  13.0 0.0 copy-start.3
  13.0 12.4 %all-to-all-start = ((bf16[64,3072,24]{1,2,0:T(8,128)(2,1)}), bf16[64,3072,24]{1,2,0:T(8,128)(2,1)}, u32[]{:S(2)}, u32[]{:S(2)}) async-start(bf16[64,3072,24]{1,2,0:T(8,128)(2,1)} %stack.3), calls=%async_computation | async-start | bytes 18874368 | tf_op jit(solution)/shard_map/all_to_all | solution.py:39
  25.4 0.0 all-gather.3.cloned.1.call-start
  25.5 0.7 all-gather.3.cloned.1.call-update
  26.2 0.0 copy-done.3
  26.2 0.1 copy.15
  26.3 0.1 reduce-window.8
  26.4 0.1 reduce.5
  26.5 0.0 copy-done.2
  26.5 0.1 convert_reduce_fusion.1
  26.6 0.1 select_reduce_fusion
  26.7 0.0 copy-done
  26.7 0.1 convert_reduce_fusion
  26.9 0.3 fusion.23
  27.2 0.0 copy-done.1
  27.2 0.3 fusion.21
  27.5 234.1 %all-to-all-done = bf16[64,3072,24]{1,2,0:T(8,128)(2,1)} async-done(((bf16[64,3072,24]{1,2,0:T(8,128)(2,1)}), bf16[64,3072,24]{1,2,0:T(8,128)(2,1)}, u32[]{:S(2)}, u32[]{:S(2)}) %all-to-all-start) | async-done | bytes 9437216 | tf_op jit(solution)/shard_map/all_to_all | solution.py:39
  261.7 1.3 collective-permute-start
  263.0 10.1 %collective-permute-done = bf16[128,1536]{1,0:T(8,128)(2,1)S(1)} collective-permute-done((bf16[128,1536]{1,0:T(8,128)(2,1)S(1)}, bf16[128,1536]{1,0:T(8,128)(2,1)S(1)}, u32[]{:S(2)}, u32[]{:S(2)}) %collective-permute-start) | collective-permute-done | bytes 393248 | tf_op jit(solution)/shard_map/ppermute | solution.py:13
  273.1 1.3 collective-permute-start.1
  274.4 9.2 %collective-permute-done.1 = bf16[128,1536]{1,0:T(8,128)(2,1)S(1)} collective-permute-done((bf16[128,1536]{1,0:T(8,128)(2,1)S(1)}, bf16[128,1536]{1,0:T(8,128)(2,1)S(1)}, u32[]{:S(2)}, u32[]{:S(2)}) %collective-permute-start.1) | collective-permute-done | bytes 393248 | tf_op jit(solution)/shard_map/ppermute | solution.py:13
  283.6 1.3 collective-permute-start.2
  284.9 64.5 %collective-permute-done.2 = bf16[128,1536]{1,0:T(8,128)(2,1)S(1)} collective-permute-done((bf16[128,1536]{1,0:T(8,128)(2,1)S(1)}, bf16[128,1536]{1,0:T(8,128)(2,1)S(1)}, u32[]{:S(2)}, u32[]{:S(2)}) %collective-permute-start.2) | collective-permute-done | bytes 393248 | tf_op jit(solution)/shard_map/ppermute | solution.py:13
  349.4 20.4 %conditional.7 = (bf16[128,1536]{1,0:T(8,128)(2,1)S(1)}, f32[1536]{0:T(1024)S(1)}) conditional(s32[]{:T(128)} %convert_element_type.77, bf16[128,1536]{1,0:T(8,128)(2,1)S(1)} %collective-permute-done.2, (bf16[128,1536]{1,0:T(8,128)(2,1)S(1)}, f32[128,1]{0,1:T(1,128)S(1)}, bf16[3072,1536]{0,1:T(8,128)(2,1)}, bf16[128,1536]{1,0:T(8,128)(2,1)S(1)}, ...), branch_computations={%region_20.21_spmd, %region_21.25_spmd} | conditional | flops 3630562048 | bytes 36211220 | solution.py:77
  349.4 6.2 %fusion.28 = f32[128,3072]{1,0:T(8,128)} fusion(bf16[128,1536]{1,0:T(8,128)(2,1)S(1)} %get-tuple-element.84, bf16[1536,3072]{1,0:T(8,128)(2,1)} %get-tuple-element.85), kind=kOutput, calls=%fused_computation.69 | convolution fusion | flops 1207959552 | bytes 11403264 | tf_op jit(solution)/shard_map/cond/branch_1_fun/dot_general | solution.py:44
  355.7 12.7 %multiply_reduce_fusion.9 = (f32[1536]{0:T(1024)S(1)}, f32[128]{0:T(128)S(1)}, f32[128]{0:T(128)S(1)}, f32[128,1536]{1,0:T(8,128)}) fusion(f32[128,1536]{1,0:T(8,128)S(1)} %get-tuple-element.87, f32[1536]{0:T(1024)S(1)} %reduce.4, bf16[1536,3072]{1,0:T(8,128)(2,1)} %get-tuple-element.85, bf16[128,1536]{1,0:T(8,128)(2,1)S(1)} %get-tuple-element.81, ...), kind=kOutput, calls=%fused_computation.39 | convolution fusion | flops 2421029376 | bytes 22426624 | tf_op jit(solution)/shard_map/cond/branch_1_fun/dot_general | solution.py:48
  368.4 1.4 add_convert_fusion.3
  369.8 2.5 psum.21
  372.3 11.6 %psum.22 = f32[1536]{0:T(1024)S(1)} all-reduce(f32[1536]{0:T(1024)S(1)} %psum.21), channel_id=1, replica_groups=mesh['segment'=4,'z'=8,'y'=4,'core'=2] {'y'}, use_global_device_ids=true, to_apply=%region_26.27 | all-reduce | flops 1536 | bytes 12288 | tf_op jit(solution)/shard_map/psum | solution.py:82
  383.9 20.7 %psum.23 = f32[1,1536]{1,0:T(1,128)} all-reduce(f32[1,1536]{1,0:T(1,128)S(1)} %broadcast_in_dim.5), channel_id=1, replica_groups=mesh['segment'=4,'z'=8,'y'=4,'core'=2] {'z'}, use_global_device_ids=true, to_apply=%region_27.28 | all-reduce | flops 1536 | bytes 12288 | tf_op jit(solution)/shard_map/psum | solution.py:82
  404.6 0.8 select_bitcast_fusion
  (20 shorter events, 0.2 us)
Async XLA Ops:
  13.0 13.2 %copy-start.3 = (s32[64]{0:T(128)S(1)}, s32[64]{0:T(128)}, u32[]{:S(2)}) copy-start(s32[64]{0:T(128)} %param.19) | copy-start | bytes 772
  13.0 13.5 %copy-start.2 = (f32[1,1536]{1,0:T(1,128)S(1)}, f32[1,1536]{1,0:T(1,128)}, u32[]{:S(2)}) copy-start(f32[1,1536]{1,0:T(1,128)} %param.15) | copy-start | bytes 18436
  13.0 13.7 %copy-start = (bf16[1,128,1536]{2,1,0:T(8,128)(2,1)S(1)}, bf16[1,128,1536]{2,1,0:T(8,128)(2,1)}, u32[]{:S(2)}) copy-start(bf16[1,128,1536]{2,1,0:T(8,128)(2,1)} %param.14) | copy-start | bytes 1179652
  13.0 14.2 %copy-start.1 = (bf16[128,1536]{1,0:T(8,128)(2,1)S(1)}, bf16[128,1536]{1,0:T(8,128)(2,1)}, u32[]{:S(2)}) copy-start(bf16[128,1536]{1,0:T(8,128)(2,1)} %param.18) | copy-start | bytes 1179652
  13.0 248.7 %all-to-all-start = ((bf16[64,3072,24]{1,2,0:T(8,128)(2,1)}), bf16[64,3072,24]{1,2,0:T(8,128)(2,1)}, u32[]{:S(2)}, u32[]{:S(2)}) async-start(bf16[64,3072,24]{1,2,0:T(8,128)(2,1)} %stack.3), calls=%async_computation | async-start | bytes 18874368 | tf_op jit(solution)/shard_map/all_to_all | solution.py:39
  25.4 236.2 %all-gather.3.cloned.1.call-start = ((), (), s32[]{:S(2)}) async-start(), calls=%async_computation.1 | async-start | bytes 9584640 | tf_op jit(solution)/shard_map/all_gather | solution.py:37
  261.7 11.4 %collective-permute-start = (bf16[128,1536]{1,0:T(8,128)(2,1)S(1)}, bf16[128,1536]{1,0:T(8,128)(2,1)S(1)}, u32[]{:S(2)}, u32[]{:S(2)}) collective-permute-start(bf16[128,1536]{1,0:T(8,128)(2,1)S(1)} %get-tuple-element.98), channel_id=1, source_target_pairs={{64,0},{128,64},{192,128},{65,1},{129,65},{193,129},{66,2},{130,66... | collective-permute-start | bytes 1179656 | tf_op jit(solution)/shard_map/ppermute | solution.py:13
  273.1 10.5 %collective-permute-start.1 = (bf16[128,1536]{1,0:T(8,128)(2,1)S(1)}, bf16[128,1536]{1,0:T(8,128)(2,1)S(1)}, u32[]{:S(2)}, u32[]{:S(2)}) collective-permute-start(bf16[128,1536]{1,0:T(8,128)(2,1)S(1)} %get-tuple-element.99), channel_id=1, source_target_pairs={{64,0},{128,64},{192,128},{65,1},{129,65},{193,129},{66,2},{130,66... | collective-permute-start | bytes 1179656 | tf_op jit(solution)/shard_map/ppermute | solution.py:13
  283.6 65.8 %collective-permute-start.2 = (bf16[128,1536]{1,0:T(8,128)(2,1)S(1)}, bf16[128,1536]{1,0:T(8,128)(2,1)S(1)}, u32[]{:S(2)}, u32[]{:S(2)}) collective-permute-start(bf16[128,1536]{1,0:T(8,128)(2,1)S(1)} %get-tuple-element.100), channel_id=1, source_target_pairs={{64,0},{128,64},{192,128},{65,1},{129,65},{193,129},{66,2},{130,66... | collective-permute-start | bytes 1179656 | tf_op jit(solution)/shard_map/ppermute | solution.py:13
Sparse Core Ops, SparseCore 0:
  29.0 151.9 all-gather.2
